TPU v7x, 32 devices: a whole 2x2x4 slice. The times are simulated.
32 devices in a mesh: section: 4 (over x, core), sp: 2 (over y), rep: 4 (over z).
Axes of the slice: x: 2, y: 2, z: 4, core: 2. Of those that a mesh axis runs over, the one named last changes fastest.
Arguments:
- tokens: float32 [2, 2, 24, 3072], P('sp', None, 'section', 'rep'), may hold values from -120 to 120
- mod_scale: float32 [3072], replicated, may hold values from -3 to 3
- mod_shift: float32 [3072], replicated, may hold values from -3 to 3
- proj_weight: float32 [64, 3072], replicated, may hold values from -0.109375 to 0.109375
- proj_bias: float32 [64], replicated, may hold values from -3 to 3
- noisy_latent: float32 [2, 4, 48, 16], P(None, 'sp', 'section'), may hold values from -120 to 120
- in_weight: float32 [3, 3, 3, 16, 512], replicated, may hold values from -0.3125 to 0.3125
- in_bias: float32 [512], replicated, may hold values from -3 to 3
- conv_weight: bfloat16 [3, 3, 3, 256, 512], P(None, None, None, 'rep'), may hold values from -0.0546875 to 0.0546875
- conv_bias: float32 [256], P('rep'), may hold values from -3 to 3
- norm_gain: float32 [256], P('rep'), may hold values from 0.25 to 1.75
- norm_bias: float32 [256], P('rep'), may hold values from -3 to 3
Outputs:
- decoded: float32 [8, 96, 512], P('sp', 'section', 'rep')
All inputs are finite; a program needn't handle non-finite values.
Results may differ from a plain program's by a relative error of at most 0.0026.
Values sent between devices are 32-bit elements; how exact they have to be, the bound alone decides.
No kernel may reach another device: no remote copies, remote signals or barrier semaphores. Data moves between devices by JAX's collectives and lax.ppermute only.
A program may use at most 64 MiB of HBM per device.

v0:
```python
import jax
import jax.numpy as jnp
from jax import lax
from jax.sharding import PartitionSpec as P

D = 3072
LC = 16
CO = 256
GROUPS = 32


def with_halo(block, sides, width):
    for axis, dim in sides:
        count = lax.axis_size(axis)
        forward = [(i, i + 1) for i in range(count - 1)]
        backward = [(target, source) for source, target in forward]
        low = lax.ppermute(
            lax.slice_in_dim(block, block.shape[dim] - width, None, axis=dim), axis, forward
        )
        high = lax.ppermute(lax.slice_in_dim(block, 0, width, axis=dim), axis, backward)
        block = jnp.concatenate([low, block, high], axis=dim)
    return block


def valid_conv(volume, kernel, kernel_spec, precision_mode):
    front = jnp.concatenate([volume[:1], volume[:1], volume], axis=0)
    result = lax.conv_general_dilated(
        front[None],
        kernel,
        (1, 1, 1),
        "VALID",
        dimension_numbers=("NDHWC", kernel_spec, "NDHWC"),
        precision=precision_mode,
        preferred_element_type=jnp.float32,
    )
    return result[0]


def per_device(
    tokens,
    mod_scale,
    mod_shift,
    proj_weight,
    proj_bias,
    noisy_latent,
    in_weight,
    in_bias,
    conv_weight,
    conv_bias,
    norm_gain,
    norm_bias,
):
    local_width = tokens.shape[-1]
    scaled_weight = proj_weight * (1.0 + mod_scale)[None, :]
    center_column = jnp.sum(scaled_weight, axis=1)
    shift_column = (
        jnp.dot(
            proj_weight,
            mod_shift,
            precision=lax.Precision.HIGHEST,
            preferred_element_type=jnp.float32,
        )
        + proj_bias
    )
    local_weight = lax.dynamic_slice_in_dim(
        scaled_weight, lax.axis_index("rep") * local_width, local_width, 1
    )
    moved_tokens = lax.all_to_all(tokens, "sp", split_axis=1, concat_axis=0, tiled=True)
    projected = lax.dot_general(
        moved_tokens,
        local_weight,
        (((3,), (1,)), ((), ())),
        precision=lax.Precision.HIGHEST,
        preferred_element_type=jnp.float32,
    )
    projected, first_sums, square_sums = (
        projected,
        jnp.sum(moved_tokens, axis=-1),
        jnp.sum(moved_tokens * moved_tokens, axis=-1),
    )
    projected, first_sums, square_sums = lax.psum((projected, first_sums, square_sums), "rep")
    token_mean = first_sums / D
    token_var = square_sums / D - token_mean * token_mean
    velocity = (
        lax.rsqrt(token_var + 1e-06)[..., None]
        * (projected - token_mean[..., None] * center_column)
        + shift_column
    )
    frames, slab_rows, band_cols = (velocity.shape[0], velocity.shape[1], velocity.shape[2])
    patches = (
        velocity.reshape(frames, slab_rows, band_cols, LC, 2, 2)
        .transpose(0, 1, 4, 2, 5, 3)
        .reshape(frames, 2 * slab_rows, 2 * band_cols, LC)
    )
    clean = noisy_latent - 0.5 * patches
    extended = with_halo(clean, (("section", 2), ("sp", 1)), 2)
    inner_features = valid_conv(extended, in_weight, "DHWIO", lax.Precision.HIGHEST) + in_bias
    latent_rows = 2 * slab_rows
    latent_cols = 2 * band_cols
    row_global = lax.axis_index("sp") * latent_rows - 1 + jnp.arange(latent_rows + 2)
    col_global = lax.axis_index("section") * latent_cols - 1 + jnp.arange(latent_cols + 2)
    row_inside = (row_global >= 0) & (row_global < latent_rows * lax.axis_size("sp"))
    col_inside = (col_global >= 0) & (col_global < latent_cols * lax.axis_size("section"))
    inside = row_inside[None, :, None, None] & col_inside[None, None, :, None]
    features = jnp.where(inside, inner_features, 0.0).astype(jnp.bfloat16)
    upsampled = jnp.repeat(jnp.repeat(features, 2, axis=1), 2, axis=2)[:, 1:-1, 1:-1, :]
    mixed = valid_conv(upsampled, conv_weight, "DHWOI", None) + conv_bias
    group_size = CO // GROUPS
    local_groups = mixed.shape[-1] // group_size
    grouped = mixed.reshape(-1, local_groups, group_size)
    cell_count = grouped.shape[0] * group_size * lax.axis_size("section") * lax.axis_size("sp")
    group_mean = lax.psum(jnp.sum(grouped, axis=(0, 2)), ("section", "sp")) / cell_count
    deviation = grouped - group_mean[None, :, None]
    group_var = (
        lax.psum(jnp.sum(deviation * deviation, axis=(0, 2)), ("section", "sp")) / cell_count
    )
    normed = (
        (grouped - group_mean[None, :, None]) * lax.rsqrt(group_var + 1e-06)[None, :, None]
    ).reshape(mixed.shape)
    activated = jax.nn.silu(normed * norm_gain + norm_bias)
    out_rows, out_cols, out_chan = (activated.shape[1], activated.shape[2], activated.shape[3])
    return activated.transpose(1, 2, 3, 0).reshape(out_rows, out_cols, out_chan * frames)


def solution(mesh):
    return jax.shard_map(
        per_device,
        mesh=mesh,
        in_specs=(
            P("sp", None, "section", "rep"),
            P(),
            P(),
            P(),
            P(),
            P(None, "sp", "section", None),
            P(),
            P(),
            P(None, None, None, "rep", None),
            P("rep"),
            P("rep"),
            P("rep"),
        ),
        out_specs=P("sp", "section", "rep"),
        check_vma=False,
    )
```

profile of v0, /device:TPU:0, one launch (start us, length us, event | category | flops | bytes accessed | tf_op | source)
XLA Modules:
  0.0 79.5 jit_solution(5452324065720546734)
XLA Ops:
  0.0 0.0 copy-start
  0.0 0.0 copy-start.2
  0.0 1.6 %copy.53 = f32[1,2,6,768]{3,0,2,1:T(1,128)} copy(f32[1,2,6,768]{3,1,2,0:T(2,128)} %param.12) | data formatting | bytes 73728 | tf_op args[0]
  1.6 4.2 %all-to-all-start = ((f32[1,2,6,768]{3,0,2,1:T(1,128)}), f32[1,2,6,768]{3,0,2,1:T(1,128)S(1)}, u32[]{:S(2)}, u32[]{:S(2)}) async-start(f32[1,2,6,768]{3,0,2,1:T(1,128)} %copy.53), calls=%async_computation | async-start | bytes 73728 | tf_op jit(solution)/shard_map/all_to_all | solution.py:68
  5.8 0.7 broadcast_add_fusion
  6.5 1.3 %fusion.37 = (f32[64]{0:T(128)S(1)}, f32[64,3072]{1,0:T(8,128)S(1)}) fusion(f32[64,3072]{1,0:T(8,128)} %param.15, f32[3072]{0:T(1024)S(1)} %broadcast_add_fusion), kind=kLoop, calls=%fused_computation.63 | loop fusion | flops 393152 | bytes 1585408 | tf_op jit(solution)/shard_map/reduce_sum | solution.py:55
  7.9 0.0 copy-start.10
  7.9 0.0 copy-done.1
  7.9 0.0 copy-done.6
  7.9 0.0 copy-done.3
  7.9 0.7 fusion.11
  8.7 1.1 %all-to-all-done = f32[1,2,6,768]{3,0,2,1:T(1,128)S(1)} async-done(((f32[1,2,6,768]{3,0,2,1:T(1,128)}), f32[1,2,6,768]{3,0,2,1:T(1,128)S(1)}, u32[]{:S(2)}, u32[]{:S(2)}) %all-to-all-start) | async-done | bytes 36896 | tf_op jit(solution)/shard_map/all_to_all | solution.py:68
  9.8 0.2 convolution_bitcast_fusion
  10.1 0.2 multiply_reduce_fusion
  10.3 19.4 %all-reduce = (f32[2,1,6,64]{3,2,0,1:T(8,128)S(1)}, f32[2,1,6]{2,0,1:T(2,128)S(1)}, f32[2,1,6]{2,0,1:T(2,128)S(1)}) all-reduce(f32[2,1,6,64]{3,2,0,1:T(8,128)S(1)} %convolution_bitcast_fusion, f32[2,1,6]{2,0,1:T(2,128)S(1)} %bitcast.85, f32[2,1,6]{2,0,1:T(2,128)S(1)} %bitcast.84), channel_id=1, replica_groups=mesh['section'=4,'sp'=2,'rep'=4] {'rep'}, use_global_device_ids=true, to_apply=%region_4.0 | all-reduce | flops 792 | bytes 6336 | tf_op jit(solution)/shard_map/psum | solution.py:81
  29.7 0.1 add_multiply_fusion
  29.8 0.1 copy.56
  29.9 0.1 copy.57
  30.0 0.0 copy-done.2
  30.1 1.3 %collective-permute-start = (f32[2,2,2,16]{3,1,2,0:T(2,128)S(1)}, f32[2,2,2,16]{3,1,2,0:T(2,128)S(1)}, u32[]{:S(2)}, u32[]{:S(2)}) collective-permute-start(f32[2,2,2,16]{3,1,2,0:T(2,128)S(1)} %get-tuple-element.12), channel_id=1, source_target_pairs={{0,8},{8,16},{16,24},{1,9},{9,17},{17,25},{2,10},{10,18},{18,26},{... | collective-permute-start | bytes 1544 | tf_op jit(solution)/shard_map/ppermute | solution.py:17
  31.4 1.3 %collective-permute-start.1 = (f32[2,2,2,16]{3,1,2,0:T(2,128)S(1)}, f32[2,2,2,16]{3,1,2,0:T(2,128)S(1)}, u32[]{:S(2)}, u32[]{:S(2)}) collective-permute-start(f32[2,2,2,16]{3,1,2,0:T(2,128)S(1)} %get-tuple-element.13), channel_id=1, source_target_pairs={{8,0},{16,8},{24,16},{9,1},{17,9},{25,17},{10,2},{18,10},{26,18},{... | collective-permute-start | bytes 1544 | tf_op jit(solution)/shard_map/ppermute | solution.py:20
  32.7 0.0 collective-permute-done
  32.7 3.5 %collective-permute-done.1 = f32[2,2,2,16]{3,1,2,0:T(2,128)S(1)} collective-permute-done((f32[2,2,2,16]{3,1,2,0:T(2,128)S(1)}, f32[2,2,2,16]{3,1,2,0:T(2,128)S(1)}, u32[]{:S(2)}, u32[]{:S(2)}) %collective-permute-start.1) | collective-permute-done | bytes 544 | tf_op jit(solution)/shard_map/ppermute | solution.py:20
  36.2 1.3 %collective-permute-start.3 = (f32[2,2,16,16]{3,1,2,0:T(2,128)S(1)}, f32[2,2,16,16]{3,1,2,0:T(2,128)S(1)}, u32[]{:S(2)}, u32[]{:S(2)}) collective-permute-start(f32[2,2,16,16]{3,1,2,0:T(2,128)S(1)} %pad_maximum_fusion.4), channel_id=1, source_target_pairs={{4,0},{5,1},{6,2},{7,3},{12,8},{13,9},{14,10},{15,11},{20,16},{21,... | collective-permute-start | bytes 12296 | tf_op jit(solution)/shard_map/ppermute | solution.py:20
  37.5 4.5 %collective-permute-start.2 = (f32[2,2,16,16]{3,1,2,0:T(2,128)S(1)}, f32[2,2,16,16]{3,1,2,0:T(2,128)S(1)}, u32[]{:S(2)}, u32[]{:S(2)}) collective-permute-start(f32[2,2,16,16]{3,1,2,0:T(2,128)S(1)} %pad_maximum_fusion.4), channel_id=1, source_target_pairs={{0,4},{1,5},{2,6},{3,7},{8,12},{9,13},{10,14},{11,15},{16,20},{17,... | collective-permute-start | bytes 12296 | tf_op jit(solution)/shard_map/ppermute | solution.py:17
  42.1 0.1 broadcast_and_fusion
  42.1 0.0 collective-permute-done.3
  42.1 1.5 %collective-permute-done.2 = f32[2,2,16,16]{3,1,2,0:T(2,128)S(1)} collective-permute-done((f32[2,2,16,16]{3,1,2,0:T(2,128)S(1)}, f32[2,2,16,16]{3,1,2,0:T(2,128)S(1)}, u32[]{:S(2)}, u32[]{:S(2)}) %collective-permute-start.2) | collective-permute-done | bytes 4128 | tf_op jit(solution)/shard_map/ppermute | solution.py:17
  43.7 0.1 maximum_maximum_fusion
  43.8 0.0 copy-start.4
  43.9 2.8 %convolution_select_fusion = f32[2,4,8,2,512]{4,2,3,1,0:T(8,128)S(1)} fusion(f32[3,3,3,16,512]{4,3,2,1,0:T(8,128)} %param.18, f32[4,6,1,7,2,16]{5,3,4,1,0,2:T(8,128)S(1)} %slice.29, f32[4,6,1,8,2,16]{5,3,4,1,0,2:T(8,128)S(1)} %copy.60, pred[8,2]{0,1:T(4,128)(4,1)S(1)} %copy-done.10), kind=kOutput, calls=%fused_computation.8 | convolution fusion | flops 339841024 | bytes 1192976 | tf_op jit(solution)/shard_map/conv_general_dilated | solution.py:27
  46.7 0.2 copy.61
  46.9 0.1 fusion.19
  47.0 0.1 broadcast_in_dim.23
  47.1 0.1 reshape.129
  47.3 0.1 slice.31
  47.3 0.1 slice.32
  47.4 0.2 maximum_bitcast_fusion
  47.6 0.5 copy.68
  48.1 0.0 copy-start.5
  48.1 0.0 copy-start.9
  48.2 0.3 pad.1.clone
  48.4 0.4 copy.64
  48.9 0.1 slice.33
  49.0 0.0 copy-done
  49.0 0.0 copy-done.5
  49.0 0.0 copy-done.9
  49.0 0.0 copy-start.7
  49.0 0.0 copy-start.8
  49.0 2.0 %select_reduce_fusion.1 = (f32[64]{0:T(128)S(1)}, f32[2,4,8,4,64]{4,2,3,1,0:T(8,128)S(1)}) fusion(f32[64]{0:T(128)S(1)} %copy-done.5, pred[8,4]{0,1:T(4,128)(4,1)S(1)} %copy-done.9, bf16[3,3,3,64,512]{4,3,2,1,0:T(8,128)(2,1)S(1)} %copy-done, bf16[4,6,1,7,2,512]{5,3,4,1,0,2:T(8,128)(2,1)S(1)} %slice.33, bf16[4,6,1,8,4,512]{5,3,4,1,0,2:T(8,128)(2,1)S(1)} %copy.64), kind=kOutput, calls=%fused_computation.31 | convolution fusion | flops 456589248 | bytes 2966048 | tf_op jit(solution)/shard_map/conv_general_dilated | solution.py:27
  51.0 0.1 reduce_sum.69
  51.1 0.1 reduce_sum.70
  51.2 14.4 %psum.38 = f32[8]{0:T(128)S(1)} all-reduce(f32[8]{0:T(128)S(1)} %reduce_sum.70), channel_id=1, replica_groups=mesh['section'=4,'sp'=2,'rep'=4] {'section','sp'}, use_global_device_ids=true, to_apply=%region_8.9 | all-reduce | flops 8 | bytes 64 | tf_op jit(solution)/shard_map/psum | solution.py:112
  65.7 0.1 sub.42
  65.7 0.1 sub.43
  65.8 0.1 select_reduce_fusion
  65.9 0.1 reduce_sum.72
  66.0 0.1 reduce_sum.73
  66.2 12.2 %psum.39 = f32[8]{0:T(128)S(1)} all-reduce(f32[8]{0:T(128)S(1)} %reduce_sum.73), channel_id=1, replica_groups=mesh['section'=4,'sp'=2,'rep'=4] {'section','sp'}, use_global_device_ids=true, to_apply=%region_11.12 | all-reduce | flops 8 | bytes 64 | tf_op jit(solution)/shard_map/psum | solution.py:115
  78.4 0.1 mul.129
  78.5 0.1 mul.130
  78.6 0.1 multiply_bitcast_fusion
  78.7 0.2 copy.66
  78.8 0.7 copy.67
  (22 shorter events, 0.3 us)
Async XLA Ops:
  0.0 49.0 %copy-start = (bf16[3,3,3,64,512]{4,3,2,1,0:T(8,128)(2,1)S(1)}, bf16[3,3,3,64,512]{4,3,2,1,0:T(8,128)(2,1)}, u32[]{:S(2)}) copy-start(bf16[3,3,3,64,512]{4,3,2,1,0:T(8,128)(2,1)} %param.20) | copy-start | bytes 5308420
  0.0 7.9 %copy-start.1 = (f32[64,3072]{1,0:T(8,128)S(1)}, f32[64,3072]{1,0:T(8,128)}, u32[]{:S(2)}) copy-start(f32[64,3072]{1,0:T(8,128)} %param.15) | copy-start | bytes 2359300
  0.0 7.9 %copy-start.6 = (f32[64]{0:T(128)S(1)}, f32[64]{0:T(128)}, u32[]{:S(2)}) copy-start(f32[64]{0:T(128)} %param.16) | copy-start | bytes 772
  0.0 7.9 %copy-start.3 = (f32[3072]{0:T(1024)S(1)}, f32[3072]{0:T(1024)}, u32[]{:S(2)}) copy-start(f32[3072]{0:T(1024)} %param.14) | copy-start | bytes 36868
  0.0 30.0 %copy-start.2 = (f32[2,2,12,16]{3,1,2,0:T(2,128)S(1)}, f32[2,2,12,16]{3,1,2,0:T(2,128)}, u32[]{:S(2)}) copy-start(f32[2,2,12,16]{3,1,2,0:T(2,128)} %param.17) | copy-start | bytes 9220
  1.6 8.2 %all-to-all-start = ((f32[1,2,6,768]{3,0,2,1:T(1,128)}), f32[1,2,6,768]{3,0,2,1:T(1,128)S(1)}, u32[]{:S(2)}, u32[]{:S(2)}) async-start(f32[1,2,6,768]{3,0,2,1:T(1,128)} %copy.53), calls=%async_computation | async-start | bytes 73728 | tf_op jit(solution)/shard_map/all_to_all | solution.py:68
  7.9 36.0 %copy-start.10 = (pred[8,2]{0,1:T(4,128)(4,1)S(1)}, pred[8,2]{0,1:T(4,128)(4,1)}, u32[]{:S(2)}) copy-start(pred[8,2]{0,1:T(4,128)(4,1)} %constant.62) | copy-start | bytes 52
  30.1 2.6 %collective-permute-start = (f32[2,2,2,16]{3,1,2,0:T(2,128)S(1)}, f32[2,2,2,16]{3,1,2,0:T(2,128)S(1)}, u32[]{:S(2)}, u32[]{:S(2)}) collective-permute-start(f32[2,2,2,16]{3,1,2,0:T(2,128)S(1)} %get-tuple-element.12), channel_id=1, source_target_pairs={{0,8},{8,16},{16,24},{1,9},{9,17},{17,25},{2,10},{10,18},{18,26},{... | collective-permute-start | bytes 1544 | tf_op jit(solution)/shard_map/ppermute | solution.py:17
  31.4 4.8 %collective-permute-start.1 = (f32[2,2,2,16]{3,1,2,0:T(2,128)S(1)}, f32[2,2,2,16]{3,1,2,0:T(2,128)S(1)}, u32[]{:S(2)}, u32[]{:S(2)}) collective-permute-start(f32[2,2,2,16]{3,1,2,0:T(2,128)S(1)} %get-tuple-element.13), channel_id=1, source_target_pairs={{8,0},{16,8},{24,16},{9,1},{17,9},{25,17},{10,2},{18,10},{26,18},{... | collective-permute-start | bytes 1544 | tf_op jit(solution)/shard_map/ppermute | solution.py:20
  36.2 5.9 %collective-permute-start.3 = (f32[2,2,16,16]{3,1,2,0:T(2,128)S(1)}, f32[2,2,16,16]{3,1,2,0:T(2,128)S(1)}, u32[]{:S(2)}, u32[]{:S(2)}) collective-permute-start(f32[2,2,16,16]{3,1,2,0:T(2,128)S(1)} %pad_maximum_fusion.4), channel_id=1, source_target_pairs={{4,0},{5,1},{6,2},{7,3},{12,8},{13,9},{14,10},{15,11},{20,16},{21,... | collective-permute-start | bytes 12296 | tf_op jit(solution)/shard_map/ppermute | solution.py:20
  37.5 6.1 %collective-permute-start.2 = (f32[2,2,16,16]{3,1,2,0:T(2,128)S(1)}, f32[2,2,16,16]{3,1,2,0:T(2,128)S(1)}, u32[]{:S(2)}, u32[]{:S(2)}) collective-permute-start(f32[2,2,16,16]{3,1,2,0:T(2,128)S(1)} %pad_maximum_fusion.4), channel_id=1, source_target_pairs={{0,4},{1,5},{2,6},{3,7},{8,12},{9,13},{10,14},{11,15},{16,20},{17,... | collective-permute-start | bytes 12296 | tf_op jit(solution)/shard_map/ppermute | solution.py:17
  43.8 3.0 %copy-start.4 = (f32[512]{0:T(512)S(1)}, f32[512]{0:T(512)}, u32[]{:S(2)}) copy-start(f32[512]{0:T(512)} %param.19) | copy-start | bytes 6148
  48.1 0.9 %copy-start.5 = (f32[64]{0:T(128)S(1)}, f32[64]{0:T(128)}, u32[]{:S(2)}) copy-start(f32[64]{0:T(128)} %param.21) | copy-start | bytes 772
  48.1 0.9 %copy-start.9 = (pred[8,4]{0,1:T(4,128)(4,1)S(1)}, pred[8,4]{0,1:T(4,128)(4,1)}, u32[]{:S(2)}) copy-start(pred[8,4]{0,1:T(4,128)(4,1)} %constant.61) | copy-start | bytes 100
  49.0 29.6 %copy-start.7 = (f32[64]{0:T(128)S(1)}, f32[64]{0:T(128)}, u32[]{:S(2)}) copy-start(f32[64]{0:T(128)} %param.23) | copy-start | bytes 772
  49.0 29.6 %copy-start.8 = (f32[64]{0:T(128)S(1)}, f32[64]{0:T(128)}, u32[]{:S(2)}) copy-start(f32[64]{0:T(128)} %param.22) | copy-start | bytes 772
where the time goes:
time: 80 us; the launch traced here: 79.5 us
  blocking collectives  46.1 us (58%)
  starting transfers between devices  12.7 us (16%)
  waiting for transfers between devices  6.12 us (8%)
  matrix products  5.79 us (7%)
  local copies, waits for them, and re-layouts  5.24 us (7%)
  other arithmetic  3.28 us (4%)
    psum x1, blocking collectives, per_device(): lax.psum((projected, first_sums, square_sums), 'rep')  19.4 us
    psum x1, blocking collectives, per_device(): lax.psum(jnp.sum(grouped, axis=(0, 2)), ('section', 'sp')) / cell_count  14.4 us
    psum x1, blocking collectives, per_device(): lax.psum(jnp.sum(deviation * deviation, axis=(0, 2)), ('section', 'sp'))  12.2 us
    ppermute x2, starting transfers between devices, with_halo(): lax.ppermute(lax.slice_in_dim(block, block.shape[dim] - width, None, axis...  5.84 us
    conv_general_dilated x2, matrix products, valid_conv(): lax.conv_general_dilated(front[None], kernel, (1, 1, 1), 'VALID', dimensi...  4.83 us
    all_to_all x1, starting transfers between devices, per_device(): lax.all_to_all(tokens, 'sp', split_axis=1, concat_axis=0, tiled=True)  4.24 us
    ppermute x2, waiting for transfers between devices, with_halo(): lax.ppermute(lax.slice_in_dim(block, 0, width, axis=dim), axis, backward)  3.47 us
    ppermute x2, starting transfers between devices, with_halo(): lax.ppermute(lax.slice_in_dim(block, 0, width, axis=dim), axis, backward)  2.58 us
  transfers between devices with their start and end apart: 5, of which 3 were waited for; matrix products, arithmetic and copies ran while one was open for 4% of the time, Pallas kernels for 0%

commit v1 on v0

--- a/solution.py
+++ b/solution.py
@@ -65,7 +65,10 @@
     local_weight = lax.dynamic_slice_in_dim(
         scaled_weight, lax.axis_index("rep") * local_width, local_width, 1
     )
-    moved_tokens = lax.all_to_all(tokens, "sp", split_axis=1, concat_axis=0, tiled=True)
+    moved_tokens = jnp.concatenate(
+        lax.all_to_all(jnp.stack(jnp.split(tokens, lax.axis_size("sp"), axis=1)), "sp", 0, 0),
+        axis=0,
+    )
     projected = lax.dot_general(
         moved_tokens,
         local_weight,

time: 80 us -> 80.1 us (level)
    unnamed x24 -> x23, local copies, waits for them, and re-layouts: 2.13 us -> 0.56 us
    another operation x0 -> x1, local copies, waits for them, and re-layouts: none -> 0.97 us  [per_device(): jnp.stack(jnp.split(tokens, lax.axis_size('sp'), axis=1))]
where the time goes in v1:
time: 80.1 us; the launch traced here: 79.6 us
  blocking collectives  46.1 us (58%)
  starting transfers between devices  12.7 us (16%)
  waiting for transfers between devices  6.12 us (8%)
  matrix products  5.85 us (7%)
  local copies, waits for them, and re-layouts  4.64 us (6%)
  other arithmetic  3.88 us (5%)
    psum x1, blocking collectives, per_device(): lax.psum((projected, first_sums, square_sums), 'rep')  19.4 us
    psum x1, blocking collectives, per_device(): lax.psum(jnp.sum(grouped, axis=(0, 2)), ('section', 'sp')) / cell_count  14.4 us
    psum x1, blocking collectives, per_device(): lax.psum(jnp.sum(deviation * deviation, axis=(0, 2)), ('section', 'sp'))  12.2 us
    ppermute x2, starting transfers between devices, with_halo(): lax.ppermute(lax.slice_in_dim(block, block.shape[dim] - width, None, axis...  5.84 us
    conv_general_dilated x2, matrix products, valid_conv(): lax.conv_general_dilated(front[None], kernel, (1, 1, 1), 'VALID', dimensi...  4.83 us
    all_to_all x1, starting transfers between devices, per_device(): lax.all_to_all(jnp.stack(jnp.split(tokens, lax.axis_size('sp'), axis=1)),...  4.24 us
    ppermute x2, waiting for transfers between devices, with_halo(): lax.ppermute(lax.slice_in_dim(block, 0, width, axis=dim), axis, backward)  3.47 us
    ppermute x2, starting transfers between devices, with_halo(): lax.ppermute(lax.slice_in_dim(block, 0, width, axis=dim), axis, backward)  2.58 us
  transfers between devices with their start and end apart: 5, of which 3 were waited for; matrix products, arithmetic and copies ran while one was open for 4% of the time, Pallas kernels for 0%

profile of v1, /device:TPU:0, one launch (start us, length us, event | category | flops | bytes accessed | tf_op | source)
XLA Modules:
  0.0 79.6 jit_solution(3037994450119333057)
XLA Ops:
  0.0 0.0 copy-start
  0.0 0.0 copy-start.2
  0.0 1.0 %slice_bitcast_fusion.3 = (f32[1,1,1,6,768]{4,2,3,1,0:T(1,128)S(1)}, f32[1,1,1,6,768]{4,2,3,1,0:T(1,128)S(1)}) fusion(f32[1,2,6,768]{3,1,2,0:T(2,128)} %param.12), kind=kLoop, calls=%fused_computation.49 | loop fusion | bytes 73728 | tf_op jit(solution)/shard_map/stack | solution.py:69
  1.0 0.7 pad_maximum_fusion.4
  1.6 4.2 %all-to-all-start = ((f32[2,1,1,6,768]{4,2,3,1,0:T(1,128)}), f32[2,1,1,6,768]{4,2,3,1,0:T(1,128)S(1)}, u32[]{:S(2)}, u32[]{:S(2)}) async-start(f32[2,1,1,6,768]{4,2,3,1,0:T(1,128)} %pad_maximum_fusion.4), calls=%async_computation | async-start | bytes 73728 | tf_op jit(solution)/shard_map/all_to_all | solution.py:69
  5.9 0.7 broadcast_add_fusion
  6.6 1.3 %fusion.37 = (f32[64]{0:T(128)S(1)}, f32[64,3072]{1,0:T(8,128)S(1)}) fusion(f32[64,3072]{1,0:T(8,128)} %param.15, f32[3072]{0:T(1024)S(1)} %broadcast_add_fusion), kind=kLoop, calls=%fused_computation.66 | loop fusion | flops 393152 | bytes 1585408 | tf_op jit(solution)/shard_map/reduce_sum | solution.py:55
  7.9 0.0 copy-start.10
  7.9 0.0 copy-done.1
  8.0 0.7 fusion.11
  8.7 1.1 %all-to-all-done = f32[2,1,1,6,768]{4,2,3,1,0:T(1,128)S(1)} async-done(((f32[2,1,1,6,768]{4,2,3,1,0:T(1,128)}), f32[2,1,1,6,768]{4,2,3,1,0:T(1,128)S(1)}, u32[]{:S(2)}, u32[]{:S(2)}) %all-to-all-start) | async-done | bytes 36896 | tf_op jit(solution)/shard_map/all_to_all | solution.py:69
  9.9 0.3 convolution_bitcast_fusion
  10.2 0.2 multiply_reduce_fusion
  10.3 19.4 %all-reduce = (f32[2,1,6,64]{3,2,0,1:T(8,128)S(1)}, f32[2,1,6]{2,0,1:T(2,128)S(1)}, f32[2,1,6]{2,0,1:T(2,128)S(1)}) all-reduce(f32[2,1,6,64]{3,2,0,1:T(8,128)S(1)} %convolution_bitcast_fusion, f32[2,1,6]{2,0,1:T(2,128)S(1)} %bitcast.91, f32[2,1,6]{2,0,1:T(2,128)S(1)} %bitcast.90), channel_id=1, replica_groups=mesh['section'=4,'sp'=2,'rep'=4] {'rep'}, use_global_device_ids=true, to_apply=%region_4.0 | all-reduce | flops 792 | bytes 6336 | tf_op jit(solution)/shard_map/psum | solution.py:84
  29.8 0.1 add_multiply_fusion
  29.9 0.1 copy.61
  30.0 0.1 copy.62
  30.1 0.0 copy-done.2
  30.1 1.3 %collective-permute-start = (f32[2,2,2,16]{3,1,2,0:T(2,128)S(1)}, f32[2,2,2,16]{3,1,2,0:T(2,128)S(1)}, u32[]{:S(2)}, u32[]{:S(2)}) collective-permute-start(f32[2,2,2,16]{3,1,2,0:T(2,128)S(1)} %get-tuple-element.14), channel_id=1, source_target_pairs={{0,8},{8,16},{16,24},{1,9},{9,17},{17,25},{2,10},{10,18},{18,26},{... | collective-permute-start | bytes 1544 | tf_op jit(solution)/shard_map/ppermute | solution.py:17
  31.4 1.3 %collective-permute-start.1 = (f32[2,2,2,16]{3,1,2,0:T(2,128)S(1)}, f32[2,2,2,16]{3,1,2,0:T(2,128)S(1)}, u32[]{:S(2)}, u32[]{:S(2)}) collective-permute-start(f32[2,2,2,16]{3,1,2,0:T(2,128)S(1)} %get-tuple-element.15), channel_id=1, source_target_pairs={{8,0},{16,8},{24,16},{9,1},{17,9},{25,17},{10,2},{18,10},{26,18},{... | collective-permute-start | bytes 1544 | tf_op jit(solution)/shard_map/ppermute | solution.py:20
  32.8 0.0 collective-permute-done
  32.8 3.5 %collective-permute-done.1 = f32[2,2,2,16]{3,1,2,0:T(2,128)S(1)} collective-permute-done((f32[2,2,2,16]{3,1,2,0:T(2,128)S(1)}, f32[2,2,2,16]{3,1,2,0:T(2,128)S(1)}, u32[]{:S(2)}, u32[]{:S(2)}) %collective-permute-start.1) | collective-permute-done | bytes 544 | tf_op jit(solution)/shard_map/ppermute | solution.py:20
  36.3 1.3 %collective-permute-start.3 = (f32[2,2,16,16]{3,1,2,0:T(2,128)S(1)}, f32[2,2,16,16]{3,1,2,0:T(2,128)S(1)}, u32[]{:S(2)}, u32[]{:S(2)}) collective-permute-start(f32[2,2,16,16]{3,1,2,0:T(2,128)S(1)} %pad_maximum_fusion.5), channel_id=1, source_target_pairs={{4,0},{5,1},{6,2},{7,3},{12,8},{13,9},{14,10},{15,11},{20,16},{21,... | collective-permute-start | bytes 12296 | tf_op jit(solution)/shard_map/ppermute | solution.py:20
  37.6 4.5 %collective-permute-start.2 = (f32[2,2,16,16]{3,1,2,0:T(2,128)S(1)}, f32[2,2,16,16]{3,1,2,0:T(2,128)S(1)}, u32[]{:S(2)}, u32[]{:S(2)}) collective-permute-start(f32[2,2,16,16]{3,1,2,0:T(2,128)S(1)} %pad_maximum_fusion.5), channel_id=1, source_target_pairs={{0,4},{1,5},{2,6},{3,7},{8,12},{9,13},{10,14},{11,15},{16,20},{17,... | collective-permute-start | bytes 12296 | tf_op jit(solution)/shard_map/ppermute | solution.py:17
  42.1 0.1 broadcast_and_fusion
  42.2 0.0 collective-permute-done.3
  42.2 1.5 %collective-permute-done.2 = f32[2,2,16,16]{3,1,2,0:T(2,128)S(1)} collective-permute-done((f32[2,2,16,16]{3,1,2,0:T(2,128)S(1)}, f32[2,2,16,16]{3,1,2,0:T(2,128)S(1)}, u32[]{:S(2)}, u32[]{:S(2)}) %collective-permute-start.2) | collective-permute-done | bytes 4128 | tf_op jit(solution)/shard_map/ppermute | solution.py:17
  43.7 0.1 maximum_maximum_fusion
  43.9 0.0 copy-start.4
  43.9 2.8 %convolution_select_fusion = f32[2,4,8,2,512]{4,2,3,1,0:T(8,128)S(1)} fusion(f32[3,3,3,16,512]{4,3,2,1,0:T(8,128)} %param.18, f32[4,6,1,7,2,16]{5,3,4,1,0,2:T(8,128)S(1)} %slice.29, f32[4,6,1,8,2,16]{5,3,4,1,0,2:T(8,128)S(1)} %copy.65, pred[8,2]{0,1:T(4,128)(4,1)S(1)} %copy-done.10), kind=kOutput, calls=%fused_computation.8 | convolution fusion | flops 339841024 | bytes 1192976 | tf_op jit(solution)/shard_map/conv_general_dilated | solution.py:27
  46.7 0.2 copy.66
  46.9 0.1 fusion.19
  47.1 0.1 broadcast_in_dim.23
  47.2 0.1 reshape.127
  47.3 0.1 slice.31
  47.4 0.1 slice.32
  47.5 0.2 maximum_bitcast_fusion
  47.7 0.5 copy.75
  48.2 0.0 copy-start.5
  48.2 0.0 copy-start.9
  48.2 0.3 pad.1.clone
  48.5 0.4 copy.69
  48.9 0.1 slice.33
  49.0 0.0 copy-done
  49.1 0.0 copy-done.5
  49.1 0.0 copy-done.9
  49.1 0.0 copy-start.7
  49.1 0.0 copy-start.8
  49.1 2.0 %select_reduce_fusion.1 = (f32[64]{0:T(128)S(1)}, f32[2,4,8,4,64]{4,2,3,1,0:T(8,128)S(1)}) fusion(f32[64]{0:T(128)S(1)} %copy-done.5, pred[8,4]{0,1:T(4,128)(4,1)S(1)} %copy-done.9, bf16[3,3,3,64,512]{4,3,2,1,0:T(8,128)(2,1)S(1)} %copy-done, bf16[4,6,1,7,2,512]{5,3,4,1,0,2:T(8,128)(2,1)S(1)} %slice.33, bf16[4,6,1,8,4,512]{5,3,4,1,0,2:T(8,128)(2,1)S(1)} %copy.69), kind=kOutput, calls=%fused_computation.31 | convolution fusion | flops 456589248 | bytes 2966048 | tf_op jit(solution)/shard_map/conv_general_dilated | solution.py:27
  51.1 0.1 reduce_sum.69
  51.2 0.1 reduce_sum.70
  51.3 14.4 %psum.38 = f32[8]{0:T(128)S(1)} all-reduce(f32[8]{0:T(128)S(1)} %reduce_sum.70), channel_id=1, replica_groups=mesh['section'=4,'sp'=2,'rep'=4] {'section','sp'}, use_global_device_ids=true, to_apply=%region_8.9 | all-reduce | flops 8 | bytes 64 | tf_op jit(solution)/shard_map/psum | solution.py:115
  65.7 0.1 sub.42
  65.8 0.1 sub.43
  65.9 0.1 select_reduce_fusion
  66.0 0.1 reduce_sum.72
  66.1 0.1 reduce_sum.73
  66.2 12.2 %psum.39 = f32[8]{0:T(128)S(1)} all-reduce(f32[8]{0:T(128)S(1)} %reduce_sum.73), channel_id=1, replica_groups=mesh['section'=4,'sp'=2,'rep'=4] {'section','sp'}, use_global_device_ids=true, to_apply=%region_11.12 | all-reduce | flops 8 | bytes 64 | tf_op jit(solution)/shard_map/psum | solution.py:118
  78.5 0.1 mul.129
  78.6 0.1 mul.130
  78.6 0.0 copy-done.7
  78.7 0.1 multiply_bitcast_fusion
  78.7 0.2 copy.71
  78.9 0.7 copy.72
  (23 shorter events, 0.3 us)
Async XLA Ops:
  0.0 49.0 %copy-start = (bf16[3,3,3,64,512]{4,3,2,1,0:T(8,128)(2,1)S(1)}, bf16[3,3,3,64,512]{4,3,2,1,0:T(8,128)(2,1)}, u32[]{:S(2)}) copy-start(bf16[3,3,3,64,512]{4,3,2,1,0:T(8,128)(2,1)} %param.20) | copy-start | bytes 5308420
  0.0 7.9 %copy-start.1 = (f32[64,3072]{1,0:T(8,128)S(1)}, f32[64,3072]{1,0:T(8,128)}, u32[]{:S(2)}) copy-start(f32[64,3072]{1,0:T(8,128)} %param.15) | copy-start | bytes 2359300
  0.0 7.9 %copy-start.6 = (f32[64]{0:T(128)S(1)}, f32[64]{0:T(128)}, u32[]{:S(2)}) copy-start(f32[64]{0:T(128)} %param.16) | copy-start | bytes 772
  0.0 7.9 %copy-start.3 = (f32[3072]{0:T(1024)S(1)}, f32[3072]{0:T(1024)}, u32[]{:S(2)}) copy-start(f32[3072]{0:T(1024)} %param.14) | copy-start | bytes 36868
  0.0 30.1 %copy-start.2 = (f32[2,2,12,16]{3,1,2,0:T(2,128)S(1)}, f32[2,2,12,16]{3,1,2,0:T(2,128)}, u32[]{:S(2)}) copy-start(f32[2,2,12,16]{3,1,2,0:T(2,128)} %param.17) | copy-start | bytes 9220
  1.6 8.2 %all-to-all-start = ((f32[2,1,1,6,768]{4,2,3,1,0:T(1,128)}), f32[2,1,1,6,768]{4,2,3,1,0:T(1,128)S(1)}, u32[]{:S(2)}, u32[]{:S(2)}) async-start(f32[2,1,1,6,768]{4,2,3,1,0:T(1,128)} %pad_maximum_fusion.4), calls=%async_computation | async-start | bytes 73728 | tf_op jit(solution)/shard_map/all_to_all | solution.py:69
  7.9 36.0 %copy-start.10 = (pred[8,2]{0,1:T(4,128)(4,1)S(1)}, pred[8,2]{0,1:T(4,128)(4,1)}, u32[]{:S(2)}) copy-start(pred[8,2]{0,1:T(4,128)(4,1)} %constant.62) | copy-start | bytes 52
  30.1 2.6 %collective-permute-start = (f32[2,2,2,16]{3,1,2,0:T(2,128)S(1)}, f32[2,2,2,16]{3,1,2,0:T(2,128)S(1)}, u32[]{:S(2)}, u32[]{:S(2)}) collective-permute-start(f32[2,2,2,16]{3,1,2,0:T(2,128)S(1)} %get-tuple-element.14), channel_id=1, source_target_pairs={{0,8},{8,16},{16,24},{1,9},{9,17},{17,25},{2,10},{10,18},{18,26},{... | collective-permute-start | bytes 1544 | tf_op jit(solution)/shard_map/ppermute | solution.py:17
  31.4 4.8 %collective-permute-start.1 = (f32[2,2,2,16]{3,1,2,0:T(2,128)S(1)}, f32[2,2,2,16]{3,1,2,0:T(2,128)S(1)}, u32[]{:S(2)}, u32[]{:S(2)}) collective-permute-start(f32[2,2,2,16]{3,1,2,0:T(2,128)S(1)} %get-tuple-element.15), channel_id=1, source_target_pairs={{8,0},{16,8},{24,16},{9,1},{17,9},{25,17},{10,2},{18,10},{26,18},{... | collective-permute-start | bytes 1544 | tf_op jit(solution)/shard_map/ppermute | solution.py:20
  36.3 5.9 %collective-permute-start.3 = (f32[2,2,16,16]{3,1,2,0:T(2,128)S(1)}, f32[2,2,16,16]{3,1,2,0:T(2,128)S(1)}, u32[]{:S(2)}, u32[]{:S(2)}) collective-permute-start(f32[2,2,16,16]{3,1,2,0:T(2,128)S(1)} %pad_maximum_fusion.5), channel_id=1, source_target_pairs={{4,0},{5,1},{6,2},{7,3},{12,8},{13,9},{14,10},{15,11},{20,16},{21,... | collective-permute-start | bytes 12296 | tf_op jit(solution)/shard_map/ppermute | solution.py:20
  37.6 6.1 %collective-permute-start.2 = (f32[2,2,16,16]{3,1,2,0:T(2,128)S(1)}, f32[2,2,16,16]{3,1,2,0:T(2,128)S(1)}, u32[]{:S(2)}, u32[]{:S(2)}) collective-permute-start(f32[2,2,16,16]{3,1,2,0:T(2,128)S(1)} %pad_maximum_fusion.5), channel_id=1, source_target_pairs={{0,4},{1,5},{2,6},{3,7},{8,12},{9,13},{10,14},{11,15},{16,20},{17,... | collective-permute-start | bytes 12296 | tf_op jit(solution)/shard_map/ppermute | solution.py:17
  43.9 3.0 %copy-start.4 = (f32[512]{0:T(512)S(1)}, f32[512]{0:T(512)}, u32[]{:S(2)}) copy-start(f32[512]{0:T(512)} %param.19) | copy-start | bytes 6148
  48.2 0.9 %copy-start.5 = (f32[64]{0:T(128)S(1)}, f32[64]{0:T(128)}, u32[]{:S(2)}) copy-start(f32[64]{0:T(128)} %param.21) | copy-start | bytes 772
  48.2 0.9 %copy-start.9 = (pred[8,4]{0,1:T(4,128)(4,1)S(1)}, pred[8,4]{0,1:T(4,128)(4,1)}, u32[]{:S(2)}) copy-start(pred[8,4]{0,1:T(4,128)(4,1)} %constant.61) | copy-start | bytes 100
  49.1 29.6 %copy-start.7 = (f32[64]{0:T(128)S(1)}, f32[64]{0:T(128)}, u32[]{:S(2)}) copy-start(f32[64]{0:T(128)} %param.23) | copy-start | bytes 772
  49.1 29.6 %copy-start.8 = (f32[64]{0:T(128)S(1)}, f32[64]{0:T(128)}, u32[]{:S(2)}) copy-start(f32[64]{0:T(128)} %param.22) | copy-start | bytes 772
